TPU v7x, 512 devices: a whole 4x8x8 slice. The times are simulated.
512 devices in a mesh: row: 32 (over z_hi, y), col: 16 (over x, z_lo, core).
Axes of the slice: x: 4, y: 8, z: 8 (z_hi: 4, z_lo: 2; z = z_hi * 2 + z_lo), core: 2. Of those that a mesh axis runs over, the one named last changes fastest.
Arguments:
- s_rows: bfloat16 [32768, 1024], P('row', 'col'), may hold values from -0.1875 to 0.1875
- iterate: bfloat16 [1024, 32768], P('row', 'col'), may hold values from -6 to 6
Outputs:
- product: bfloat16 [32768, 32768], P('row', 'col')
All inputs are finite; a program needn't handle non-finite values.
Results may differ from a plain program's by a relative error of at most 0.001.
Values may be sent and summed in bfloat16 or wider, within the bound.
No kernel may reach another device: no remote copies, remote signals or barrier semaphores. Data moves between devices by JAX's collectives and lax.ppermute only.
A program may use at most 64 MiB of HBM per device.

v0:
```python
import jax
import jax.numpy as jnp
from jax import lax
from jax.sharding import Mesh, PartitionSpec as P

ROW = ("z_hi", "y")
COL = ("x", "z_lo", "core")


def shards(s_rows, iterate):
    panel = lax.all_gather(s_rows, COL, axis=1, tiled=True)
    nz, ny = (lax.axis_size("z_hi"), lax.axis_size("y"))
    w = lax.all_gather(iterate, "z_hi", axis=0, tiled=False)
    w = lax.all_gather(w, "y", axis=0, tiled=False)
    s4 = panel.reshape(panel.shape[0], nz, ny, -1)
    product = jnp.einsum("rzyk,yzkc->rc", s4, w, preferred_element_type=jnp.float32)
    return product.astype(jnp.bfloat16)


def solution(mesh):
    nr, nc = mesh.devices.shape
    devs = mesh.devices.reshape(4, nr // 4, nc // 4, 2, 2)
    m = Mesh(devs, ROW + COL)
    return jax.shard_map(
        shards, mesh=m, in_specs=(P(ROW, COL), P(ROW, COL)), out_specs=P(ROW, COL), check_vma=False
    )
```

profile of v0, /device:TPU:1, one launch (start us, length us, event | category | flops | bytes accessed | tf_op | source)
XLA Modules:
  0.0 129.2 jit_solution(9073005861399664550)
XLA Ops:
  6.5 0.0 all-gather.5.cloned.1.call-start
  6.5 0.7 all-gather.5.cloned.1.call-update
  7.3 0.0 all-gather.7.cloned.1.call-start
  7.3 21.6 %all-gather = bf16[128,2048]{1,0:T(8,128)(2,1)} all-gather(bf16[32,2048]{1,0:T(8,128)(2,1)} %param.3), channel_id=2, replica_groups=mesh['z_hi'=4,'y'=8,'x'=4,'z_lo'=2,'core'=2] {'z_hi'}, dimensions={0}, use_global_device_ids=true | all-gather | bytes 655360 | tf_op jit(solution)/shard_map/all_gather | solution.py:13
  28.9 0.0 all-gather.7.cloned.1.call-update
  28.9 25.8 %all-gather.5.cloned.1.call-done = bf16[1024,1024]{0,1:T(8,128)(2,1)} async-done(((bf16[1024,64]{0,1:T(8,128)(2,1)}), bf16[1024,1024]{0,1:T(8,128)(2,1)}) %all-gather.5.cloned.1.call-update) | async-done | bytes 2097168 | tf_op jit(solution)/shard_map/all_gather | solution.py:11
  54.7 58.3 %all-gather.7.cloned.1.call-done = bf16[32,32,2048]{2,1,0:T(8,128)(2,1)} async-done(((bf16[4,32,2048]{2,1,0:T(8,128)(2,1)}), bf16[32,32,2048]{2,1,0:T(8,128)(2,1)}) %all-gather.7.cloned.1.call-update) | async-done | bytes 4194320 | tf_op jit(solution)/shard_map/all_gather | solution.py:14
  113.0 9.4 %bitcast_convert_fusion = bf16[1024,2048]{1,0:T(8,128)(2,1)} fusion(bf16[8,4,32,2048]{3,2,1,0:T(8,128)(2,1)} %bitcast.9, bf16[1024,4,8,32]{0,3,2,1:T(8,128)(2,1)} %bitcast.10), kind=kOutput, calls=%fused_computation | convolution fusion | flops 4297064448 | bytes 10485760 | tf_op jit(solution)/shard_map/rzyk,yzkc->rc/dot_general | solution.py:16
Async XLA Ops:
  6.5 48.2 %all-gather.5.cloned.1.call-start = ((), (), s32[]{:S(2)}) async-start(), calls=%async_computation | async-start | bytes 2228224 | tf_op jit(solution)/shard_map/all_gather | solution.py:11
  7.3 105.7 %all-gather.7.cloned.1.call-start = ((), (), s32[]{:S(2)}) async-start(), calls=%async_computation.1 | async-start | bytes 4718592 | tf_op jit(solution)/shard_map/all_gather | solution.py:14
Sparse Core Ops, SparseCore 0:
  9.5 45.1 all-gather.4
  56.8 56.1 all-gather.6
where the time goes:
time: 129 us
  waiting for transfers between devices  84.8 us (66%)
  blocking collectives  21.6 us (17%)
  between operations  13.4 us (10%)
  matrix products  9.41 us (7%)
    all_gather x1, waiting for transfers between devices, shards(): w = lax.all_gather(w, 'y', axis=0, tiled=False)  58.3 us
    all_gather x1, waiting for transfers between devices, shards(): panel = lax.all_gather(s_rows, COL, axis=1, tiled=True)  25.8 us
    all_gather x1, blocking collectives, shards(): w = lax.all_gather(iterate, 'z_hi', axis=0, tiled=False)  21.6 us
    dot_general x1, matrix products, shards(): jnp.einsum('rzyk,yzkc->rc', s4, w, preferred_element_type=jnp.float32)  9.41 us
  transfers between devices with their start and end apart: 2, of which 2 were waited for; matrix products, arithmetic and copies ran while one was open for 0% of the time, Pallas kernels for 0%

commit v1 on v0

--- a/solution.py
+++ b/solution.py
@@ -7,8 +7,17 @@
 COL = ("x", "z_lo", "core")
 
 
+def sizes_guide(unit):
+    nodes = []
+    for _ in range(lax.axis_size(COL)):
+        nodes.append(unit)
+    u1 = jnp.stack(nodes)
+    local_next = lax.all_to_all(u1, COL, split_axis=0, concat_axis=0)
+    return jnp.concatenate(local_next, axis=1)
+
+
 def shards(s_rows, iterate):
-    panel = lax.all_gather(s_rows, COL, axis=1, tiled=True)
+    panel = sizes_guide(s_rows)
     nz, ny = (lax.axis_size("z_hi"), lax.axis_size("y"))
     w = lax.all_gather(iterate, "z_hi", axis=0, tiled=False)
     w = lax.all_gather(w, "y", axis=0, tiled=False)

time: 129 us -> 102 us (0.79)
  waiting for transfers between devices: 84.8 us -> 22.2 us
  blocking collectives: 21.6 us -> 57.2 us
    all_gather x1, waiting for transfers between devices: 58.3 us -> 22.2 us  [shards(): w = lax.all_gather(w, 'y', axis=0, tiled=False)]
    all_to_all x0 -> x1, blocking collectives: none -> 35.7 us  [sizes_guide(): local_next = lax.all_to_all(u1, COL, split_axis=0, concat_axis=0)]
    all_gather x1 -> x0, waiting for transfers between devices: 25.8 us -> none  [shards(): panel = lax.all_gather(s_rows, COL, axis=1, tiled=True)]
  transfers between devices with their start and end apart: 2 -> 1, of which waited for: 2 -> 1; matrix products, arithmetic and copies ran while one was open for 0% -> 1% of each run, Pallas kernels for 0% -> 0%
where the time goes in v1:
time: 102 us
  blocking collectives  57.2 us (56%)
  waiting for transfers between devices  22.2 us (22%)
  between operations  13.4 us (13%)
  matrix products  8.31 us (8%)
  local copies, waits for them, and re-layouts  1.16 us (1%)
    all_to_all x1, blocking collectives, sizes_guide(): local_next = lax.all_to_all(u1, COL, split_axis=0, concat_axis=0)  35.7 us
    all_gather x1, waiting for transfers between devices, shards(): w = lax.all_gather(w, 'y', axis=0, tiled=False)  22.2 us
    all_gather x1, blocking collectives, shards(): w = lax.all_gather(iterate, 'z_hi', axis=0, tiled=False)  21.6 us
    dot_general x1, matrix products, shards(): jnp.einsum('rzyk,yzkc->rc', s4, w, preferred_element_type=jnp.float32)  8.31 us
  transfers between devices with their start and end apart: 1, of which 1 were waited for; matrix products, arithmetic and copies ran while one was open for 1% of the time, Pallas kernels for 0%

profile of v1, /device:TPU:1, one launch (start us, length us, event | category | flops | bytes accessed | tf_op | source)
XLA Modules:
  0.0 102.3 jit_solution(6217019091884960823)
XLA Ops:
  6.5 0.0 all-gather.4.cloned.1.call-start
  6.5 21.6 %all-gather = bf16[128,2048]{1,0:T(8,128)(2,1)} all-gather(bf16[32,2048]{1,0:T(8,128)(2,1)} %param.3), channel_id=2, replica_groups=mesh['z_hi'=4,'y'=8,'x'=4,'z_lo'=2,'core'=2] {'z_hi'}, dimensions={0}, use_global_device_ids=true | all-gather | bytes 655360 | tf_op jit(solution)/shard_map/all_gather | solution.py:22
  28.1 0.0 all-gather.4.cloned.1.call-update
  28.1 1.2 %stack.2 = bf16[16,1024,64]{1,2,0:T(8,128)(2,1)S(1)} broadcast(bf16[1024,64]{0,1:T(8,128)(2,1)} %param.2), dimensions={1,2} | broadcast | bytes 2228224 | tf_op jit(solution)/shard_map/stack | solution.py:14
  29.3 35.7 %all_to_all.5 = bf16[16,1024,64]{1,2,0:T(8,128)(2,1)S(1)} all-to-all(bf16[16,1024,64]{1,2,0:T(8,128)(2,1)S(1)} %stack.2), channel_id=1, replica_groups=mesh['z_hi'=4,'y'=8,'x'=4,'z_lo'=2,'core'=2] {'x','z_lo','core'}, dimensions={0} | all-to-all | bytes 4194304 | tf_op jit(solution)/shard_map/all_to_all | solution.py:15
  64.9 22.2 %all-gather.4.cloned.1.call-done = bf16[32,32,2048]{2,1,0:T(8,128)(2,1)} async-done(((bf16[4,32,2048]{2,1,0:T(8,128)(2,1)}), bf16[32,32,2048]{2,1,0:T(8,128)(2,1)}) %all-gather.4.cloned.1.call-update) | async-done | bytes 4194320 | tf_op jit(solution)/shard_map/all_gather | solution.py:23
  87.1 8.3 %bitcast_convert_fusion = bf16[1024,2048]{1,0:T(8,128)(2,1)} fusion(bf16[8,4,32,2048]{3,2,1,0:T(8,128)(2,1)} %bitcast.12, bf16[1024,4,8,32]{0,3,2,1:T(8,128)(2,1)S(1)} %bitcast.11), kind=kOutput, calls=%fused_computation | convolution fusion | flops 4297064448 | bytes 10485760 | tf_op jit(solution)/shard_map/rzyk,yzkc->rc/dot_general | solution.py:25
Async XLA Ops:
  6.5 80.6 %all-gather.4.cloned.1.call-start = ((), (), s32[]{:S(2)}) async-start(), calls=%async_computation.1 | async-start | bytes 4718592 | tf_op jit(solution)/shard_map/all_gather | solution.py:23
Sparse Core Ops, SparseCore 0:
  28.2 58.8 all-gather.3
